TPU v7x, 32 devices: a whole 2x2x4 slice. The times are simulated.
32 devices in a mesh: lat: 4 (over x, core), lon: 2 (over y), lev: 4 (over z).
Axes of the slice: x: 2, y: 2, z: 4, core: 2. Of those that a mesh axis runs over, the one named last changes fastest.
Arguments:
- fields: float32 [2, 60, 128, 256], P(None, 'lev', 'lat', 'lon'), may hold values from -6 to 6
- diffusivity: float32 [60, 128, 256], P('lev', 'lat', 'lon'), may hold values from 0.02 to 0.24
- cloudy_index: int32 [4, 2048], P('lat', 'lon'), may hold values from 0 to 4095, as said below
- owners: int32 [4, 2048, 1], P('lat', 'lon'), may hold values from 0 to 1; in each aligned block of 256 rows (0 to 255, 256 to 511, ..., all dimensions but the last counted through in order) at most 256 rows name the same one
- w_in: bfloat16 [2, 120, 1024], P('lon'), may hold values from -0.5 to 0.5
- w_mid: bfloat16 [2, 2, 1024, 1024], P('lon'), may hold values from -0.1875 to 0.1875
- w_out: bfloat16 [2, 1024, 120], P('lon'), may hold values from -0.1875 to 0.1875
Outputs:
- fields_next: float32 [2, 60, 128, 256], P(None, 'lev', 'lat', 'lon')
Inputs may be any that keep to these rules, and one draw needn't show every extreme that they name: `cloudy_index`: in row i, entries j * 1024 to (j + 1) * 1024 - 1 are distinct column numbers a * 128 + b of the dycore block (i, j). `owners`: in each aligned block of 256 rows (one level slice of one dycore block), no regime is named by more than 256 rows.
All inputs are finite; a program needn't handle non-finite values.
Results may differ from a plain program's by a relative error of at most 0.00062.
Values may be sent and summed in bfloat16 or wider, within the bound.
No kernel may reach another device: no remote copies, remote signals or barrier semaphores. Data moves between devices by JAX's collectives and lax.ppermute only.
A program may use at most 64 MiB of HBM per device.

v0:
```python
import jax
import jax.numpy as jnp
from jax import lax
from jax.sharding import PartitionSpec as P

LEVELS = 60
STEPS = 3


def halo_exchange(cells, width):
    lat_count = lax.axis_size("lat")
    from_above = lax.ppermute(
        cells[..., cells.shape[-2] - width :, :], "lat", [(i, i + 1) for i in range(lat_count - 1)]
    )
    from_below = lax.ppermute(
        cells[..., :width, :], "lat", [(i + 1, i) for i in range(lat_count - 1)]
    )
    cells = jnp.concatenate([from_above, cells, from_below], axis=-2)
    lon_count = lax.axis_size("lon")
    left = cells[..., :width]
    right = cells[..., cells.shape[-1] - width :]
    if lon_count == 2:
        both = lax.ppermute(jnp.concatenate([right, left], axis=-1), "lon", [(0, 1), (1, 0)])
        from_left, from_right = (both[..., :width], both[..., width:])
    else:
        from_left = lax.ppermute(right, "lon", [(i, (i + 1) % lon_count) for i in range(lon_count)])
        from_right = lax.ppermute(left, "lon", [((i + 1) % lon_count, i) for i in range(lon_count)])
    return jnp.concatenate([from_left, cells, from_right], axis=-1)


def substep(values, coefficients):
    centre = values[..., 1:-1, 1:-1]
    middle = coefficients[:, 1:-1, 1:-1]
    updated = centre
    for lat_cut, lon_cut in (
        (slice(0, -2), slice(1, -1)),
        (slice(2, None), slice(1, -1)),
        (slice(1, -1), slice(0, -2)),
        (slice(1, -1), slice(2, None)),
    ):
        neighbour = values[..., lat_cut, lon_cut]
        face_coef = 0.5 * (middle + coefficients[:, lat_cut, lon_cut])
        updated = updated + face_coef * (neighbour - centre)
    return updated


def clear_outside(values, rim_width, lat_rows):
    lat_pos = (
        lax.axis_index("lat") * lat_rows - rim_width + jnp.arange(values.shape[-2], dtype=jnp.int32)
    )
    inside = (lat_pos >= 0) & (lat_pos < lat_rows * lax.axis_size("lat"))
    return jnp.where(inside[:, None], values, 0.0)


def dynamics(fields, diffusivity):
    kinds, level_rows, lat_rows, lon_cols = fields.shape
    stacked = jnp.concatenate(
        [fields.reshape(kinds * level_rows, lat_rows, lon_cols), diffusivity], axis=0
    )
    stacked = halo_exchange(stacked, STEPS)
    values = stacked[: kinds * level_rows].reshape(
        kinds, level_rows, lat_rows + 2 * STEPS, lon_cols + 2 * STEPS
    )
    kappa = stacked[kinds * level_rows :]
    for repeat in range(STEPS):
        trim = repeat
        coefficients = kappa[:, trim : kappa.shape[1] - trim, trim : kappa.shape[2] - trim]
        values = substep(values, coefficients)
        rim = STEPS - repeat - 1
        if rim:
            values = clear_outside(values, rim, lat_rows)
    return values


def network(features, w_first, w_middle, w_last):
    contract = (((0,), (0,)), ((), ()))
    hidden = jax.nn.gelu(
        lax.dot_general(w_first, features, contract, preferred_element_type=jnp.float32)
    ).astype(jnp.bfloat16)
    for layer_no in range(w_middle.shape[0]):
        hidden = jax.nn.gelu(
            lax.dot_general(
                w_middle[layer_no], hidden, contract, preferred_element_type=jnp.float32
            )
        ).astype(jnp.bfloat16)
    return lax.dot_general(w_last, hidden, contract, preferred_element_type=jnp.float32).astype(
        jnp.bfloat16
    )


def on_device(fields, diffusivity, cloudy_index, owners, w_in, w_mid, w_out):
    values = dynamics(fields, diffusivity)
    lev_count = lax.axis_size("lev")
    lon_count = lax.axis_size("lon")
    level_rows = values.shape[1]
    cells = values.shape[2] * values.shape[3]
    column_ids = cloudy_index[0]
    cloudy = column_ids.shape[0]
    per_device = cloudy // lev_count
    capacity = min(per_device, 4 * per_device // lon_count)
    feature_count = 2 * LEVELS
    lat_rows, lon_cols = (values.shape[2], values.shape[3])
    local_features = 2 * level_rows
    planes = values.reshape(local_features, lat_rows, lon_cols)
    row_of = column_ids // lon_cols
    col_of = column_ids % lon_cols
    col_picker = (jnp.arange(lon_cols, dtype=jnp.int32)[:, None] == col_of[None, :]).astype(
        jnp.bfloat16
    )
    row_match = jnp.arange(lat_rows, dtype=jnp.int32)[:, None] == row_of[None, :]
    by_row = jnp.dot(
        planes.astype(jnp.bfloat16).reshape(local_features * lat_rows, lon_cols),
        col_picker,
        preferred_element_type=jnp.bfloat16,
    ).reshape(local_features, lat_rows, cloudy)
    picked = jnp.sum(jnp.where(row_match[None], by_row, jnp.zeros_like(by_row)), axis=1)
    routes = owners[0, :, 0]
    group = lon_count * lev_count
    whole_slices = capacity == per_device
    if whole_slices:
        send_buffer = jnp.broadcast_to(
            picked.reshape(local_features, 1, lev_count, per_device),
            (local_features, lon_count, lev_count, per_device),
        ).reshape(local_features, group, capacity)
    else:
        pieces = routes.reshape(lev_count, per_device)
        onehot = (pieces[:, :, None] == jnp.arange(lon_count, dtype=jnp.int32)).astype(jnp.int32)
        slot_rank = jnp.sum(jnp.cumsum(onehot, 1) * onehot, 2) - 1
        piece_of = jnp.arange(lev_count, dtype=jnp.int32)[:, None]
        slot_index = ((pieces * lev_count + piece_of) * capacity + slot_rank).reshape(cloudy)
        send_buffer = (
            jnp.zeros((local_features, group * capacity), jnp.bfloat16)
            .at[:, slot_index]
            .set(picked)
            .reshape(local_features, group, capacity)
        )
    received = lax.all_to_all(send_buffer, ("lon", "lev"), split_axis=1, concat_axis=1, tiled=True)
    inputs = (
        received.reshape(2, level_rows, lon_count, lev_count, capacity)
        .transpose(0, 3, 1, 2, 4)
        .reshape(feature_count, lon_count * capacity)
    )
    outcome = network(inputs, w_in[0], w_mid[0], w_out[0])
    outgoing = (
        outcome.reshape(2, lev_count, level_rows, lon_count, capacity)
        .transpose(0, 2, 3, 1, 4)
        .reshape(local_features, group, capacity)
    )
    returned = lax.all_to_all(outgoing, ("lon", "lev"), split_axis=1, concat_axis=1, tiled=True)
    if whole_slices:
        returned = returned.reshape(local_features, lon_count, cloudy)
        tendency = returned[:, 0]
        for regime in range(1, lon_count):
            tendency = jnp.where(routes[None, :] == regime, returned[:, regime], tendency)
    else:
        tendency = returned.reshape(local_features, group * capacity)[:, slot_index]
    spread_rows = jnp.where(
        row_match[None], tendency[:, None, :], jnp.zeros_like(tendency)[:, None, :]
    )
    spread = lax.dot_general(
        spread_rows.reshape(local_features * lat_rows, cloudy),
        col_picker,
        (((1,), (1,)), ((), ())),
        preferred_element_type=jnp.float32,
    )
    updated = planes + spread.reshape(planes.shape)
    return updated.reshape(values.shape)


def solution(mesh):
    in_specs = (
        P(None, "lev", "lat", "lon"),
        P("lev", "lat", "lon"),
        P("lat", "lon"),
        P("lat", "lon", None),
        P("lon", None, None),
        P("lon", None, None, None),
        P("lon", None, None),
    )
    out_specs = P(None, "lev", "lat", "lon")
    return jax.shard_map(
        on_device, mesh=mesh, in_specs=in_specs, out_specs=out_specs, check_vma=False
    )
```

profile of v0, /device:TPU:0, one launch (start us, length us, event | category | flops | bytes accessed | tf_op | source)
XLA Modules:
  0.0 59.5 jit_solution(7515766200177670401)
XLA Ops:
  0.0 0.0 copy-start
  0.0 1.1 %pad_maximum_fusion.16 = (f32[45,3,128]{2,1,0:T(4,128)S(1)}, f32[45,3,128]{2,1,0:T(4,128)S(1)}) fusion(f32[15,32,128]{2,1,0:T(8,128)} %param.8, f32[30,32,128]{2,1,0:T(8,128)} %bitcast.69), kind=kLoop, calls=%fused_computation.140 | loop fusion | flops 34560 | bytes 875520 | tf_op jit(solution)/shard_map/slice | solution.py:13
  1.1 1.3 %collective-permute-start.1 = (f32[45,3,128]{2,1,0:T(4,128)S(1)}, f32[45,3,128]{2,1,0:T(4,128)S(1)}, u32[]{:S(2)}, u32[]{:S(2)}) collective-permute-start(f32[45,3,128]{2,1,0:T(4,128)S(1)} %get-tuple-element.24), channel_id=1, source_target_pairs={{8,0},{16,8},{24,16},{9,1},{17,9},{25,17},{10,2},{18,10},{26,18},{... | collective-permute-start | bytes 207368 | tf_op jit(solution)/shard_map/ppermute | solution.py:15
  2.4 3.0 %collective-permute-start = (f32[45,3,128]{2,1,0:T(4,128)S(1)}, f32[45,3,128]{2,1,0:T(4,128)S(1)}, u32[]{:S(2)}, u32[]{:S(2)}) collective-permute-start(f32[45,3,128]{2,1,0:T(4,128)S(1)} %get-tuple-element.23), channel_id=1, source_target_pairs={{0,8},{8,16},{16,24},{1,9},{9,17},{17,25},{2,10},{10,18},{18,26},{... | collective-permute-start | bytes 207368 | tf_op jit(solution)/shard_map/ppermute | solution.py:12
  5.5 0.7 %and_select_fusion = (s32[1,1024]{1,0:T(1,128)S(1)}, s32[1,1024]{1,0:T(1,128)S(1)}) fusion(s32[1,1024]{1,0:T(1,128)} %param.9), kind=kLoop, calls=%fused_computation.142 | loop fusion | flops 11264 | bytes 12288 | tf_op jit(solution)/shard_map/jit(remainder)/select_n | solution.py:106
  6.2 0.7 %and_select_fusion.1 = s32[1,1024]{1,0:T(1,128)S(1)} fusion(s32[1,1024]{1,0:T(1,128)S(1)} %get-tuple-element.6, s32[1,1024]{1,0:T(1,128)} %param.9), kind=kLoop, calls=%fused_computation.144 | loop fusion | flops 12288 | bytes 12288 | tf_op jit(solution)/shard_map/jit(floor_divide)/jit(_where)/select_n | solution.py:105
  6.9 0.0 collective-permute-done.1
  6.9 0.0 collective-permute-done
  6.9 1.3 %pad_maximum_fusion.1 = f32[45,38,128]{2,1,0:T(8,128)S(1)} fusion(f32[45,3,128]{2,1,0:T(4,128)S(1)} %collective-permute-done.1, f32[15,32,128]{2,1,0:T(8,128)} %param.8, f32[30,32,128]{2,1,0:T(8,128)} %bitcast.70, f32[45,3,128]{2,1,0:T(4,128)S(1)} %collective-permute-done), kind=kLoop, calls=%fused_computation.78 | loop fusion | flops 656640 | bytes 1751040 | tf_op jit(solution)/shard_map/concatenate | solution.py:18
  8.2 0.3 fusion.118
  8.5 0.4 copy.40
  8.9 0.0 copy-start.1
  8.9 0.0 copy-start.2
  9.0 0.4 copy.39
  9.4 3.0 %collective-permute-start.2 = (f32[45,38,6]{0,1,2:T(8,128)S(1)}, f32[45,38,6]{0,1,2:T(8,128)S(1)}, u32[]{:S(2)}, u32[]{:S(2)}) collective-permute-start(f32[45,38,6]{0,1,2:T(8,128)S(1)} %pad_maximum_fusion.14), channel_id=1, source_target_pairs={{0,4},{4,0},{1,5},{5,1},{2,6},{6,2},{3,7},{7,3},{8,12},{12,8},{9,1... | collective-permute-start | bytes 123128 | tf_op jit(solution)/shard_map/ppermute | solution.py:23
  12.5 3.5 %collective-permute-done.2 = f32[45,38,6]{0,1,2:T(8,128)S(1)} collective-permute-done((f32[45,38,6]{0,1,2:T(8,128)S(1)}, f32[45,38,6]{0,1,2:T(8,128)S(1)}, u32[]{:S(2)}, u32[]{:S(2)}) %collective-permute-start.2) | collective-permute-done | bytes 41072 | tf_op jit(solution)/shard_map/ppermute | solution.py:23
  16.0 0.5 copy.52
  16.4 0.5 copy.51
  16.9 0.0 copy-done.1
  16.9 0.0 copy-done.2
  16.9 1.0 %pad_maximum_fusion = f32[45,38,134]{2,1,0:T(8,128)S(1)} fusion(f32[45,38,3]{2,1,0:T(8,128)S(1)} %copy.52, f32[45,3,128]{2,1,0:T(4,128)S(1)} %collective-permute-done.1, f32[15,32,128]{2,1,0:T(8,128)S(1)} %copy-done.2, f32[30,32,128]{2,1,0:T(8,128)S(1)} %bitcast.71, f32[45,3,128]{2,1,0:T(4,128)S(1)} %collective-permute-done, f32[45,38,3]{2,1,0:T(8,128)S(1)} %copy.51), kind=kLoop, calls=%fused_computation.37 | loop fusion | flops 1145700 | bytes 1833120 | tf_op jit(solution)/shard_map/concatenate | solution.py:28
  17.9 0.1 slice.196
  18.0 0.7 %fusion.84 = (f32[15,36,132]{2,1,0:T(8,128)S(1)}, f32[15,36,132]{2,1,0:T(8,128)S(1)}, f32[15,36,132]{2,1,0:T(8,128)S(1)}, f32[15,36,132]{2,1,0:T(8,128)S(1)}) fusion(f32[45,38,134]{2,1,0:T(8,128)S(1)} %pad_maximum_fusion), kind=kLoop, calls=%fused_computation.94 | loop fusion | flops 570240 | bytes 2566080 | tf_op jit(solution)/shard_map/mul | solution.py:42
  18.7 1.4 %fusion.44 = f32[2,15,36,132]{3,2,1,0:T(8,128)S(1)} fusion(f32[2,15,38,134]{3,2,1,0:T(8,128)S(1)} %bitcast.68, f32[15,36,132]{2,1,0:T(8,128)S(1)} %get-tuple-element.14, f32[15,36,132]{2,1,0:T(8,128)S(1)} %get-tuple-element.15, f32[15,36,132]{2,1,0:T(8,128)S(1)} %get-tuple-element.16, f32[15,36,132]{2,1,0:T(8,128)S(1)} %get-tuple-element.13, ...), kind=kLoop, calls=%fused_computation.54 | loop fusion | flops 1853280 | bytes 4561956 | tf_op jit(solution)/shard_map/jit(_where)/select_n | solution.py:52
  20.1 0.9 %fusion.80 = (f32[15,34,130]{2,1,0:T(8,128)S(1)}, f32[15,34,130]{2,1,0:T(8,128)S(1)}, f32[15,34,130]{2,1,0:T(8,128)S(1)}, f32[15,34,130]{2,1,0:T(8,128)S(1)}) fusion(f32[45,38,134]{2,1,0:T(8,128)S(1)} %pad_maximum_fusion, f32[45,38,3]{2,1,0:T(8,128)S(1)} %copy.52, f32[45,3,128]{2,1,0:T(4,128)S(1)} %collective-permute-done.1, ...), kind=kLoop, calls=%fused_computation.86 | loop fusion | flops 1060800 | bytes 2772960 | tf_op jit(solution)/shard_map/mul | solution.py:42
  21.0 1.4 %fusion.35 = f32[2,15,34,130]{3,2,1,0:T(8,128)S(1)} fusion(f32[2,15,36,132]{3,2,1,0:T(8,128)S(1)} %fusion.44, f32[15,34,130]{2,1,0:T(8,128)S(1)} %get-tuple-element.11, f32[15,34,130]{2,1,0:T(8,128)S(1)} %get-tuple-element.12, f32[15,34,130]{2,1,0:T(8,128)S(1)} %get-tuple-element.10, f32[15,34,130]{2,1,0:T(8,128)S(1)} %get-tuple-element.9, ...), kind=kLoop, calls=%fused_computation.41 | loop fusion | flops 1723800 | bytes 4243234 | tf_op jit(solution)/shard_map/jit(_where)/select_n | solution.py:52
  22.4 0.4 fusion.101
  22.8 0.6 %fusion.89 = f32[2,15,32,128]{3,2,1,0:T(8,128)S(1)} fusion(f32[2,15,34,130]{3,2,1,0:T(8,128)S(1)} %fusion.35, f32[15,32,128]{2,1,0:T(8,128)S(1)} %get-tuple-element.18, f32[15,32,128]{2,1,0:T(8,128)S(1)} %get-tuple-element.17, f32[15,32,128]{2,1,0:T(8,128)S(1)} %get-tuple-element.22, f32[15,32,128]{2,1,0:T(8,128)S(1)} %get-tuple-element.21), kind=kLoop, calls=%fused_computation.99 | loop fusion | flops 1474560 | bytes 3932160 | tf_op jit(solution)/shard_map/add | solution.py:43
  23.4 0.7 %select_reduce_fusion = bf16[30,1024]{1,0:T(8,128)(2,1)S(1)} fusion(pred[32,1024]{1,0:T(8,128)(4,1)S(1)} %iota_compare_fusion.1, bf16[30,32,128]{2,1,0:T(8,128)(2,1)S(1)} %bitcast_convert_fusion, s32[1024]{0:T(1024)S(1)} %bitcast.82), kind=kOutput, calls=%fused_computation.35 | convolution fusion | flops 253724672 | bytes 344064 | tf_op jit(solution)/shard_map/dot_general | solution.py:111
  24.2 14.3 %all_to_all.10 = bf16[30,8,256]{2,0,1:T(8,128)(2,1)S(1)} all-to-all(bf16[30,8,256]{2,0,1:T(8,128)(2,1)S(1)} %bitcast.75), channel_id=1, replica_groups=mesh['lat'=4,'lon'=2,'lev'=4] {'lon','lev'}, dimensions={1} | all-to-all | bytes 245760 | tf_op jit(solution)/shard_map/all_to_all | solution.py:137
  38.5 0.1 copy.57
  38.6 0.1 copy.45
  38.8 0.0 copy-done
  38.8 0.0 copy-start.4
  38.8 3.7 %fusion.15 = bf16[1024,512]{0,1:T(8,128)(2,1)S(1)} fusion(bf16[1,2,1024,1024]{3,2,1,0:T(8,128)(2,1)} %param.12, bf16[120,512]{1,0:T(8,128)(2,1)S(1)} %bitcast.79, bf16[1,120,1024]{2,1,0:T(8,128)(2,1)S(1)} %copy-done), kind=kOutput, calls=%fused_computation.18 | convolution fusion | flops 1209008128 | bytes 3514368 | tf_op jit(solution)/shard_map/dot_general | solution.py:82
  42.5 0.0 copy-done.4
  42.5 0.0 copy-start.3
  42.5 3.4 %fusion.64 = bf16[120,512]{1,0:T(8,128)(2,1)S(1)} fusion(bf16[1024,512]{0,1:T(8,128)(2,1)S(1)} %fusion.15, bf16[1,2,1024,1024]{3,2,1,0:T(8,128)(2,1)} %param.12, bf16[1,1024,120]{1,2,0:T(8,128)(2,1)S(1)} %copy-done.4), kind=kOutput, calls=%fused_computation.67 | convolution fusion | flops 1204350976 | bytes 3514368 | tf_op jit(solution)/shard_map/dot_general | solution.py:86
  46.1 0.7 %copy.47 = bf16[30,8,256]{2,0,1:T(8,128)(2,1)} copy(bf16[30,8,256]{2,1,0:T(8,128)(2,1)S(1)} %reshape.103) | data formatting | bytes 245760 | tf_op jit(solution)/shard_map/reshape | solution.py:147
  46.8 3.4 %all-to-all-start.1 = ((bf16[30,8,256]{2,0,1:T(8,128)(2,1)}), bf16[30,8,256]{2,0,1:T(8,128)(2,1)S(1)}, u32[]{:S(2)}, u32[]{:S(2)}) async-start(bf16[30,8,256]{2,0,1:T(8,128)(2,1)} %copy.47), calls=%async_computation.1 | async-start | bytes 262144 | tf_op jit(solution)/shard_map/all_to_all | solution.py:149
  50.2 0.0 copy-done.3
  50.2 7.4 %all-to-all-done.1 = bf16[30,8,256]{2,0,1:T(8,128)(2,1)S(1)} async-done(((bf16[30,8,256]{2,0,1:T(8,128)(2,1)}), bf16[30,8,256]{2,0,1:T(8,128)(2,1)S(1)}, u32[]{:S(2)}, u32[]{:S(2)}) %all-to-all-start.1) | async-done | bytes 122912 | tf_op jit(solution)/shard_map/all_to_all | solution.py:149
  57.6 0.1 copy.48
  57.7 0.1 reshape.104
  57.8 0.2 broadcast_select_fusion
  58.0 1.5 %fusion.51 = f32[30,32,128]{2,1,0:T(8,128)} fusion(f32[30,32,128]{2,1,0:T(8,128)S(1)} %bitcast.74, pred[32,1024]{1,0:T(8,128)(4,1)S(1)} %iota_compare_fusion.1, bf16[30,1024]{1,0:T(8,128)(2,1)S(1)} %bitcast.80, s32[1024]{0:T(1024)S(1)} %bitcast.83), kind=kOutput, calls=%fused_computation.64 | convolution fusion | flops 252895232 | bytes 1081344 | tf_op jit(solution)/shard_map/dot_general | solution.py:160
  (16 shorter events, 0.4 us)
Async XLA Ops:
  0.0 38.8 %copy-start = (bf16[1,120,1024]{2,1,0:T(8,128)(2,1)S(1)}, bf16[1,120,1024]{2,1,0:T(8,128)(2,1)}, u32[]{:S(2)}) copy-start(bf16[1,120,1024]{2,1,0:T(8,128)(2,1)} %param.11) | copy-start | bytes 737284
  1.1 5.8 %collective-permute-start.1 = (f32[45,3,128]{2,1,0:T(4,128)S(1)}, f32[45,3,128]{2,1,0:T(4,128)S(1)}, u32[]{:S(2)}, u32[]{:S(2)}) collective-permute-start(f32[45,3,128]{2,1,0:T(4,128)S(1)} %get-tuple-element.24), channel_id=1, source_target_pairs={{8,0},{16,8},{24,16},{9,1},{17,9},{25,17},{10,2},{18,10},{26,18},{... | collective-permute-start | bytes 207368 | tf_op jit(solution)/shard_map/ppermute | solution.py:15
  2.4 4.5 %collective-permute-start = (f32[45,3,128]{2,1,0:T(4,128)S(1)}, f32[45,3,128]{2,1,0:T(4,128)S(1)}, u32[]{:S(2)}, u32[]{:S(2)}) collective-permute-start(f32[45,3,128]{2,1,0:T(4,128)S(1)} %get-tuple-element.23), channel_id=1, source_target_pairs={{0,8},{8,16},{16,24},{1,9},{9,17},{17,25},{2,10},{10,18},{18,26},{... | collective-permute-start | bytes 207368 | tf_op jit(solution)/shard_map/ppermute | solution.py:12
  8.9 8.0 %copy-start.1 = (f32[2,15,32,128]{3,2,1,0:T(8,128)S(1)}, f32[2,15,32,128]{3,2,1,0:T(8,128)}, u32[]{:S(2)}) copy-start(f32[2,15,32,128]{3,2,1,0:T(8,128)} %param.7) | copy-start | bytes 1474564
  8.9 8.0 %copy-start.2 = (f32[15,32,128]{2,1,0:T(8,128)S(1)}, f32[15,32,128]{2,1,0:T(8,128)}, u32[]{:S(2)}) copy-start(f32[15,32,128]{2,1,0:T(8,128)} %param.8) | copy-start | bytes 737284
  9.4 6.6 %collective-permute-start.2 = (f32[45,38,6]{0,1,2:T(8,128)S(1)}, f32[45,38,6]{0,1,2:T(8,128)S(1)}, u32[]{:S(2)}, u32[]{:S(2)}) collective-permute-start(f32[45,38,6]{0,1,2:T(8,128)S(1)} %pad_maximum_fusion.14), channel_id=1, source_target_pairs={{0,4},{4,0},{1,5},{5,1},{2,6},{6,2},{3,7},{7,3},{8,12},{12,8},{9,1... | collective-permute-start | bytes 123128 | tf_op jit(solution)/shard_map/ppermute | solution.py:23
  38.8 3.8 %copy-start.4 = (bf16[1,1024,120]{1,2,0:T(8,128)(2,1)S(1)}, bf16[1,1024,120]{1,2,0:T(8,128)(2,1)}, u32[]{:S(2)}) copy-start(bf16[1,1024,120]{1,2,0:T(8,128)(2,1)} %param.13) | copy-start | bytes 737284
  42.5 7.7 %copy-start.3 = (s32[1,1024,1]{1,2,0:T(1,128)S(1)}, s32[1,1024,1]{1,2,0:T(1,128)}, u32[]{:S(2)}) copy-start(s32[1,1024,1]{1,2,0:T(1,128)} %param.10) | copy-start | bytes 12292
  46.8 10.8 %all-to-all-start.1 = ((bf16[30,8,256]{2,0,1:T(8,128)(2,1)}), bf16[30,8,256]{2,0,1:T(8,128)(2,1)S(1)}, u32[]{:S(2)}, u32[]{:S(2)}) async-start(bf16[30,8,256]{2,0,1:T(8,128)(2,1)} %copy.47), calls=%async_computation.1 | async-start | bytes 262144 | tf_op jit(solution)/shard_map/all_to_all | solution.py:149
where the time goes:
time: 60 us; the launch traced here: 59.5 us
  blocking collectives  14.3 us (24%)
  waiting for transfers between devices  10.9 us (18%)
  starting transfers between devices  10.7 us (18%)
  other arithmetic  10.5 us (18%)
  matrix products  9.36 us (16%)
  local copies, waits for them, and re-layouts  3.44 us (6%)
    all_to_all x1, blocking collectives, on_device(): lax.all_to_all(send_buffer, ('lon', 'lev'), split_axis=1, concat_axis=1,...  14.3 us
    all_to_all x1, waiting for transfers between devices, on_device(): lax.all_to_all(outgoing, ('lon', 'lev'), split_axis=1, concat_axis=1, til...  7.42 us
    dot_general x1, matrix products, network(): lax.dot_general(w_middle[layer_no], hidden, contract, preferred_element_t...  3.73 us
    ppermute x1, waiting for transfers between devices, halo_exchange(): lax.ppermute(jnp.concatenate([right, left], axis=-1), 'lon', [(0, 1), (1,...  3.51 us
    dot_general x1, matrix products, network(): lax.dot_general(w_last, hidden, contract, preferred_element_type=jnp.floa...  3.44 us
    all_to_all x1, starting transfers between devices, on_device(): lax.all_to_all(outgoing, ('lon', 'lev'), split_axis=1, concat_axis=1, til...  3.37 us
    ppermute x1, starting transfers between devices, halo_exchange(): lax.ppermute(cells[..., cells.shape[-2] - width:, :], 'lat', [(i, i + 1)...  3.04 us
    ppermute x1, starting transfers between devices, halo_exchange(): lax.ppermute(jnp.concatenate([right, left], axis=-1), 'lon', [(0, 1), (1,...  3.03 us
  transfers between devices with their start and end apart: 4, of which 2 were waited for; matrix products, arithmetic and copies ran while one was open for 2% of the time, Pallas kernels for 0%

commit v1 on v0

--- a/solution.py
+++ b/solution.py
@@ -5,6 +5,18 @@
 
 LEVELS = 60
 STEPS = 3
+
+
+def cycles_set(v0, dim_no, frame_in):
+    item_now, built = (v0.shape[:dim_no], v0.shape[dim_no + 1 :])
+    u1 = v0.reshape(*item_now, frame_in, -1, *built)
+    return jnp.moveaxis(u1, dim_no, 0)
+
+
+def number_results_up(message, which_dim):
+    r2 = list(message.shape[1:])
+    r2[which_dim] *= message.shape[0]
+    return jnp.moveaxis(message, 0, which_dim).reshape(r2)
 
 
 def halo_exchange(cells, width):
@@ -146,7 +158,23 @@
         .transpose(0, 2, 3, 1, 4)
         .reshape(local_features, group, capacity)
     )
-    returned = lax.all_to_all(outgoing, ("lon", "lev"), split_axis=1, concat_axis=1, tiled=True)
+
+    def attach_threads(incoming_x, axis_name, my_tile, u_in):
+        near = lax.axis_size(axis_name)
+        fresh, plain = (near, lax.axis_index(axis_name))
+        clean = cycles_set(incoming_x, my_tile, fresh)
+        cards = [clean[plain]]
+        for jj in range(1, fresh):
+            reply = clean[plain ^ jj]
+            lower = lax.ppermute(
+                reply, axis_name=axis_name, perm=[(num, num ^ jj) for num in range(fresh)]
+            )
+            cards.append(lower)
+        x_next = jnp.stack(cards, axis=0)
+        clean = x_next[plain ^ jnp.arange(fresh)]
+        return number_results_up(clean, u_in)
+
+    returned = attach_threads(outgoing, ("lon", "lev"), 1, 1)
     if whole_slices:
         returned = returned.reshape(local_features, lon_count, cloudy)
         tendency = returned[:, 0]

time: 60 us -> 64 us (1.067)
  starting transfers between devices: 10.7 us -> 25.5 us
  blocking collectives: 14.3 us -> 0 us
  waiting for transfers between devices: 10.9 us -> 13.5 us
  local copies, waits for them, and re-layouts: 3.44 us -> 4.34 us
    all_to_all x1 -> x0, blocking collectives: 14.3 us -> none  [on_device(): lax.all_to_all(send_buffer, ('lon', 'lev'), split_axis=1, concat_axis=1,...]
    ppermute x0 -> x7, starting transfers between devices: none -> 11.3 us  [attach_threads(): lax.ppermute(reply, axis_name=axis_name, perm=[(num, num ^ jj) for num in...]
    all_to_all x1, starting transfers between devices: 3.37 us -> 6.79 us  [on_device(): lax.all_to_all(send_buffer, ('lon', 'lev'), split_axis=1, concat_axis=1,...]
    ppermute x0 -> x7, waiting for transfers between devices: none -> 2.33 us  [attach_threads(): lax.ppermute(reply, axis_name=axis_name, perm=[(num, num ^ jj) for num in...]
    reshape x3 -> x0, local copies, waits for them, and re-layouts: 0.77 us -> none  [the longest x2 0.72 us: on_device(): outgoing = outcome.reshape(2, lev_count, level_rows, lon_count, capacity)...]
    broadcast_in_dim x3, local copies, waits for them, and re-layouts: 0.05 us -> 0.71 us  [on_device(): jnp.broadcast_to(picked.reshape(local_features, 1, lev_count, per_device)...]
  transfers between devices with their start and end apart: 4 -> 11, of which waited for: 2 -> 3; matrix products, arithmetic and copies ran while one was open for 2% -> 2% of each run, Pallas kernels for 0% -> 0%
where the time goes in v1:
time: 64 us; the launch traced here: 63.6 us
  starting transfers between devices  25.5 us (40%)
  waiting for transfers between devices  13.5 us (21%)
  other arithmetic  10.5 us (16%)
  matrix products  9.39 us (15%)
  local copies, waits for them, and re-layouts  4.34 us (7%)
    ppermute x7, starting transfers between devices, attach_threads(): lax.ppermute(reply, axis_name=axis_name, perm=[(num, num ^ jj) for num in...  11.3 us
    all_to_all x1, waiting for transfers between devices, on_device(): lax.all_to_all(send_buffer, ('lon', 'lev'), split_axis=1, concat_axis=1,...  7.63 us
    all_to_all x1, starting transfers between devices, on_device(): lax.all_to_all(send_buffer, ('lon', 'lev'), split_axis=1, concat_axis=1,...  6.79 us
    dot_general x1, matrix products, network(): lax.dot_general(w_middle[layer_no], hidden, contract, preferred_element_t...  3.73 us
    ppermute x1, waiting for transfers between devices, halo_exchange(): lax.ppermute(jnp.concatenate([right, left], axis=-1), 'lon', [(0, 1), (1,...  3.54 us
    dot_general x1, matrix products, network(): lax.dot_general(w_last, hidden, contract, preferred_element_type=jnp.floa...  3.48 us
    ppermute x1, starting transfers between devices, halo_exchange(): lax.ppermute(cells[..., cells.shape[-2] - width:, :], 'lat', [(i, i + 1)...  3.04 us
    ppermute x1, starting transfers between devices, halo_exchange(): lax.ppermute(jnp.concatenate([right, left], axis=-1), 'lon', [(0, 1), (1,...  3.03 us
  transfers between devices with their start and end apart: 11, of which 3 were waited for; matrix products, arithmetic and copies ran while one was open for 2% of the time, Pallas kernels for 0%

profile of v1, /device:TPU:0, one launch (start us, length us, event | category | flops | bytes accessed | tf_op | source)
XLA Modules:
  0.0 63.6 jit_solution(18341215589337476342)
XLA Ops:
  0.0 0.0 copy-start
  0.0 1.1 %pad_maximum_fusion.16 = (f32[45,3,128]{2,1,0:T(4,128)S(1)}, f32[45,3,128]{2,1,0:T(4,128)S(1)}) fusion(f32[15,32,128]{2,1,0:T(8,128)} %param.8, f32[30,32,128]{2,1,0:T(8,128)} %bitcast.116), kind=kLoop, calls=%fused_computation.141 | loop fusion | flops 34560 | bytes 875520 | tf_op jit(solution)/shard_map/slice | solution.py:25
  1.1 1.3 %collective-permute-start.1 = (f32[45,3,128]{2,1,0:T(4,128)S(1)}, f32[45,3,128]{2,1,0:T(4,128)S(1)}, u32[]{:S(2)}, u32[]{:S(2)}) collective-permute-start(f32[45,3,128]{2,1,0:T(4,128)S(1)} %get-tuple-element.24), channel_id=1, source_target_pairs={{8,0},{16,8},{24,16},{9,1},{17,9},{25,17},{10,2},{18,10},{26,18},{... | collective-permute-start | bytes 207368 | tf_op jit(solution)/shard_map/ppermute | solution.py:27
  2.4 3.0 %collective-permute-start = (f32[45,3,128]{2,1,0:T(4,128)S(1)}, f32[45,3,128]{2,1,0:T(4,128)S(1)}, u32[]{:S(2)}, u32[]{:S(2)}) collective-permute-start(f32[45,3,128]{2,1,0:T(4,128)S(1)} %get-tuple-element.23), channel_id=1, source_target_pairs={{0,8},{8,16},{16,24},{1,9},{9,17},{17,25},{2,10},{10,18},{18,26},{... | collective-permute-start | bytes 207368 | tf_op jit(solution)/shard_map/ppermute | solution.py:24
  5.5 0.7 %and_select_fusion = (s32[1,1024]{1,0:T(1,128)S(1)}, s32[1,1024]{1,0:T(1,128)S(1)}) fusion(s32[1,1024]{1,0:T(1,128)} %param.9), kind=kLoop, calls=%fused_computation.158 | loop fusion | flops 11264 | bytes 12288 | tf_op jit(solution)/shard_map/jit(remainder)/select_n | solution.py:118
  6.2 0.7 %and_select_fusion.1 = s32[1,1024]{1,0:T(1,128)S(1)} fusion(s32[1,1024]{1,0:T(1,128)S(1)} %get-tuple-element.6, s32[1,1024]{1,0:T(1,128)} %param.9), kind=kLoop, calls=%fused_computation.160 | loop fusion | flops 12288 | bytes 12288 | tf_op jit(solution)/shard_map/jit(floor_divide)/jit(_where)/select_n | solution.py:117
  6.9 0.0 collective-permute-done.1
  7.0 0.0 collective-permute-done
  7.0 1.3 %pad_maximum_fusion.1 = f32[45,38,128]{2,1,0:T(8,128)S(1)} fusion(f32[45,3,128]{2,1,0:T(4,128)S(1)} %collective-permute-done.1, f32[15,32,128]{2,1,0:T(8,128)} %param.8, f32[30,32,128]{2,1,0:T(8,128)} %bitcast.117, f32[45,3,128]{2,1,0:T(4,128)S(1)} %collective-permute-done), kind=kLoop, calls=%fused_computation.79 | loop fusion | flops 656640 | bytes 1751040 | tf_op jit(solution)/shard_map/concatenate | solution.py:30
  8.2 0.3 fusion.119
  8.5 0.4 copy.41
  9.0 0.0 copy-start.1
  9.0 0.0 copy-start.2
  9.0 0.4 copy.40
  9.5 3.0 %collective-permute-start.2 = (f32[45,38,6]{0,1,2:T(8,128)S(1)}, f32[45,38,6]{0,1,2:T(8,128)S(1)}, u32[]{:S(2)}, u32[]{:S(2)}) collective-permute-start(f32[45,38,6]{0,1,2:T(8,128)S(1)} %pad_maximum_fusion.14), channel_id=1, source_target_pairs={{0,4},{4,0},{1,5},{5,1},{2,6},{6,2},{3,7},{7,3},{8,12},{12,8},{9,1... | collective-permute-start | bytes 123128 | tf_op jit(solution)/shard_map/ppermute | solution.py:35
  12.5 3.5 %collective-permute-done.2 = f32[45,38,6]{0,1,2:T(8,128)S(1)} collective-permute-done((f32[45,38,6]{0,1,2:T(8,128)S(1)}, f32[45,38,6]{0,1,2:T(8,128)S(1)}, u32[]{:S(2)}, u32[]{:S(2)}) %collective-permute-start.2) | collective-permute-done | bytes 41072 | tf_op jit(solution)/shard_map/ppermute | solution.py:35
  16.0 0.5 copy.60
  16.5 0.5 copy.59
  17.0 0.0 copy-done.1
  17.0 0.0 copy-done.2
  17.0 1.0 %pad_maximum_fusion = f32[45,38,134]{2,1,0:T(8,128)S(1)} fusion(f32[45,38,3]{2,1,0:T(8,128)S(1)} %copy.60, f32[45,3,128]{2,1,0:T(4,128)S(1)} %collective-permute-done.1, f32[15,32,128]{2,1,0:T(8,128)S(1)} %copy-done.2, f32[30,32,128]{2,1,0:T(8,128)S(1)} %bitcast.118, f32[45,3,128]{2,1,0:T(4,128)S(1)} %collective-permute-done, f32[45,38,3]{2,1,0:T(8,128)S(1)} %copy.59), kind=kLoop, calls=%fused_computation.38 | loop fusion | flops 1145700 | bytes 1833120 | tf_op jit(solution)/shard_map/concatenate | solution.py:40
  18.0 0.1 slice.198
  18.1 0.7 %fusion.84 = (f32[15,36,132]{2,1,0:T(8,128)S(1)}, f32[15,36,132]{2,1,0:T(8,128)S(1)}, f32[15,36,132]{2,1,0:T(8,128)S(1)}, f32[15,36,132]{2,1,0:T(8,128)S(1)}) fusion(f32[45,38,134]{2,1,0:T(8,128)S(1)} %pad_maximum_fusion), kind=kLoop, calls=%fused_computation.95 | loop fusion | flops 570240 | bytes 2566080 | tf_op jit(solution)/shard_map/mul | solution.py:54
  18.8 1.4 %fusion.44 = f32[2,15,36,132]{3,2,1,0:T(8,128)S(1)} fusion(f32[2,15,38,134]{3,2,1,0:T(8,128)S(1)} %bitcast.115, f32[15,36,132]{2,1,0:T(8,128)S(1)} %get-tuple-element.14, f32[15,36,132]{2,1,0:T(8,128)S(1)} %get-tuple-element.15, f32[15,36,132]{2,1,0:T(8,128)S(1)} %get-tuple-element.16, f32[15,36,132]{2,1,0:T(8,128)S(1)} %get-tuple-element.13, ...), kind=kLoop, calls=%fused_computation.55 | loop fusion | flops 1853280 | bytes 4561956 | tf_op jit(solution)/shard_map/jit(_where)/select_n | solution.py:64
  20.2 0.9 %fusion.80 = (f32[15,34,130]{2,1,0:T(8,128)S(1)}, f32[15,34,130]{2,1,0:T(8,128)S(1)}, f32[15,34,130]{2,1,0:T(8,128)S(1)}, f32[15,34,130]{2,1,0:T(8,128)S(1)}) fusion(f32[45,38,134]{2,1,0:T(8,128)S(1)} %pad_maximum_fusion, f32[45,38,3]{2,1,0:T(8,128)S(1)} %copy.60, f32[45,3,128]{2,1,0:T(4,128)S(1)} %collective-permute-done.1, ...), kind=kLoop, calls=%fused_computation.87 | loop fusion | flops 1060800 | bytes 2772960 | tf_op jit(solution)/shard_map/mul | solution.py:54
  21.1 1.4 %fusion.35 = f32[2,15,34,130]{3,2,1,0:T(8,128)S(1)} fusion(f32[2,15,36,132]{3,2,1,0:T(8,128)S(1)} %fusion.44, f32[15,34,130]{2,1,0:T(8,128)S(1)} %get-tuple-element.11, f32[15,34,130]{2,1,0:T(8,128)S(1)} %get-tuple-element.12, f32[15,34,130]{2,1,0:T(8,128)S(1)} %get-tuple-element.10, f32[15,34,130]{2,1,0:T(8,128)S(1)} %get-tuple-element.9, ...), kind=kLoop, calls=%fused_computation.42 | loop fusion | flops 1723800 | bytes 4243234 | tf_op jit(solution)/shard_map/jit(_where)/select_n | solution.py:64
  22.5 0.4 fusion.101
  22.9 0.6 fusion.89
  23.5 0.0 copy-start.3
  23.5 0.7 %select_reduce_fusion = bf16[30,1024]{1,0:T(8,128)(2,1)S(1)} fusion(pred[32,1024]{1,0:T(8,128)(4,1)S(1)} %iota_compare_fusion.1, bf16[30,32,128]{2,1,0:T(8,128)(2,1)S(1)} %bitcast_convert_fusion, s32[1024]{0:T(1024)S(1)} %bitcast.137), kind=kOutput, calls=%fused_computation.36 | convolution fusion | flops 253724672 | bytes 344064 | tf_op jit(solution)/shard_map/dot_general | solution.py:123
  24.3 0.7 %broadcast_in_dim.102 = bf16[30,2,4,256]{3,0,2,1:T(8,128)(2,1)} broadcast(bf16[30,4,256]{2,0,1:T(8,128)(2,1)S(1)} %copy.44), dimensions={0,2,3} | broadcast | bytes 184320 | tf_op jit(solution)/shard_map/broadcast_in_dim | solution.py:133
  25.0 6.8 %all-to-all-start = ((bf16[30,8,256]{2,0,1:T(8,128)(2,1)}), bf16[30,8,256]{2,0,1:T(8,128)(2,1)S(1)}, u32[]{:S(2)}, u32[]{:S(2)}) async-start(bf16[30,8,256]{2,0,1:T(8,128)(2,1)} %bitcast.6), calls=%async_computation | async-start | bytes 262144 | tf_op jit(solution)/shard_map/all_to_all | solution.py:149
  31.8 0.0 copy-done.3
  31.8 7.6 %all-to-all-done = bf16[30,8,256]{2,0,1:T(8,128)(2,1)S(1)} async-done(((bf16[30,8,256]{2,0,1:T(8,128)(2,1)}), bf16[30,8,256]{2,0,1:T(8,128)(2,1)S(1)}, u32[]{:S(2)}, u32[]{:S(2)}) %all-to-all-start) | async-done | bytes 122912 | tf_op jit(solution)/shard_map/all_to_all | solution.py:149
  39.5 0.1 copy.73
  39.6 0.1 copy.46
  39.7 0.0 copy-done
  39.7 0.0 copy-start.4
  39.7 3.7 %fusion.15 = bf16[1024,512]{0,1:T(8,128)(2,1)S(1)} fusion(bf16[1,2,1024,1024]{3,2,1,0:T(8,128)(2,1)} %param.12, bf16[120,512]{1,0:T(8,128)(2,1)S(1)} %bitcast.127, bf16[1,120,1024]{2,1,0:T(8,128)(2,1)S(1)} %copy-done), kind=kOutput, calls=%fused_computation.19 | convolution fusion | flops 1209008128 | bytes 3514368 | tf_op jit(solution)/shard_map/dot_general | solution.py:94
  43.5 0.0 copy-done.4
  43.5 3.5 %fusion.64 = bf16[120,512]{1,0:T(8,128)(2,1)S(1)} fusion(bf16[1024,512]{0,1:T(8,128)(2,1)S(1)} %fusion.15, bf16[1,2,1024,1024]{3,2,1,0:T(8,128)(2,1)} %param.12, bf16[1,1024,120]{1,2,0:T(8,128)(2,1)S(1)} %copy-done.4), kind=kOutput, calls=%fused_computation.68 | convolution fusion | flops 1204350976 | bytes 3514368 | tf_op jit(solution)/shard_map/dot_general | solution.py:98
  47.1 0.3 constant_dynamic-slice_fusion
  47.4 0.1 collective-permute-start.3
  47.5 1.0 %collective-permute-start.4 = (bf16[30,1,256]{2,0,1:T(8,128)(2,1)S(1)}, bf16[30,1,256]{2,0,1:T(8,128)(2,1)S(1)}, u32[]{:S(2)}, u32[]{:S(2)}) collective-permute-start(bf16[30,1,256]{2,0,1:T(8,128)(2,1)S(1)} %bitcast.134), channel_id=1, source_target_pairs={{0,2},{1,3},{2,0},{3,1},{4,6},{5,7},{6,4},{7,5},{8,10},{9,11},{10,... | collective-permute-start | bytes 46088 | tf_op jit(solution)/shard_map/ppermute | solution.py:169
  48.5 3.4 %collective-permute-start.5 = (bf16[30,1,256]{2,0,1:T(8,128)(2,1)S(1)}, bf16[30,1,256]{2,0,1:T(8,128)(2,1)S(1)}, u32[]{:S(2)}, u32[]{:S(2)}) collective-permute-start(bf16[30,1,256]{2,0,1:T(8,128)(2,1)S(1)} %bitcast.133), channel_id=1, source_target_pairs={{0,3},{1,2},{2,1},{3,0},{4,7},{5,6},{6,5},{7,4},{8,11},{9,10},{10,... | collective-permute-start | bytes 46088 | tf_op jit(solution)/shard_map/ppermute | solution.py:169
  51.9 0.6 collective-permute-start.6
  52.5 0.1 collective-permute-start.7
  52.6 0.0 collective-permute-done.3
  52.6 2.1 %collective-permute-start.8 = (bf16[30,1,256]{2,0,1:T(8,128)(2,1)S(1)}, bf16[30,1,256]{2,0,1:T(8,128)(2,1)S(1)}, u32[]{:S(2)}, u32[]{:S(2)}) collective-permute-start(bf16[30,1,256]{2,0,1:T(8,128)(2,1)S(1)} %bitcast.130), channel_id=1, source_target_pairs={{0,6},{1,7},{2,4},{3,5},{4,2},{5,3},{6,0},{7,1},{8,14},{9,15},{10,... | collective-permute-start | bytes 46088 | tf_op jit(solution)/shard_map/ppermute | solution.py:169
  54.7 0.0 collective-permute-done.4
  54.8 4.0 %collective-permute-start.9 = (bf16[30,1,256]{2,0,1:T(8,128)(2,1)S(1)}, bf16[30,1,256]{2,0,1:T(8,128)(2,1)S(1)}, u32[]{:S(2)}, u32[]{:S(2)}) collective-permute-start(bf16[30,1,256]{2,0,1:T(8,128)(2,1)S(1)} %bitcast.129), channel_id=1, source_target_pairs={{0,7},{1,6},{2,5},{3,4},{4,3},{5,2},{6,1},{7,0},{8,15},{9,14},{10,... | collective-permute-start | bytes 46088 | tf_op jit(solution)/shard_map/ppermute | solution.py:169
  58.8 0.0 collective-permute-done.5
  58.8 0.0 collective-permute-done.6
  58.8 0.0 collective-permute-done.7
  58.9 0.0 collective-permute-done.8
  58.9 2.3 %collective-permute-done.9 = bf16[30,1,256]{2,0,1:T(8,128)(2,1)S(1)} collective-permute-done((bf16[30,1,256]{2,0,1:T(8,128)(2,1)S(1)}, bf16[30,1,256]{2,0,1:T(8,128)(2,1)S(1)}, u32[]{:S(2)}, u32[]{:S(2)}) %collective-permute-start.9) | collective-permute-done | bytes 15392 | tf_op jit(solution)/shard_map/ppermute | solution.py:169
  61.2 0.6 gather_fusion
  61.8 0.1 copy.48
  61.8 0.1 reshape_reshape.7
  61.9 0.2 broadcast_select_fusion
  62.1 1.5 %fusion.51 = f32[30,32,128]{2,1,0:T(8,128)} fusion(f32[30,32,128]{2,1,0:T(8,128)S(1)} %bitcast.121, pred[32,1024]{1,0:T(8,128)(4,1)S(1)} %iota_compare_fusion.1, bf16[30,1024]{1,0:T(8,128)(2,1)S(1)} %bitcast.128, s32[1024]{0:T(1024)S(1)} %bitcast.138), kind=kOutput, calls=%fused_computation.65 | convolution fusion | flops 252895232 | bytes 1081344 | tf_op jit(solution)/shard_map/dot_general | solution.py:188
  (32 shorter events, 0.4 us)
Async XLA Ops:
  0.0 39.7 %copy-start = (bf16[1,120,1024]{2,1,0:T(8,128)(2,1)S(1)}, bf16[1,120,1024]{2,1,0:T(8,128)(2,1)}, u32[]{:S(2)}) copy-start(bf16[1,120,1024]{2,1,0:T(8,128)(2,1)} %param.11) | copy-start | bytes 737284
  1.1 5.8 %collective-permute-start.1 = (f32[45,3,128]{2,1,0:T(4,128)S(1)}, f32[45,3,128]{2,1,0:T(4,128)S(1)}, u32[]{:S(2)}, u32[]{:S(2)}) collective-permute-start(f32[45,3,128]{2,1,0:T(4,128)S(1)} %get-tuple-element.24), channel_id=1, source_target_pairs={{8,0},{16,8},{24,16},{9,1},{17,9},{25,17},{10,2},{18,10},{26,18},{... | collective-permute-start | bytes 207368 | tf_op jit(solution)/shard_map/ppermute | solution.py:27
  2.4 4.6 %collective-permute-start = (f32[45,3,128]{2,1,0:T(4,128)S(1)}, f32[45,3,128]{2,1,0:T(4,128)S(1)}, u32[]{:S(2)}, u32[]{:S(2)}) collective-permute-start(f32[45,3,128]{2,1,0:T(4,128)S(1)} %get-tuple-element.23), channel_id=1, source_target_pairs={{0,8},{8,16},{16,24},{1,9},{9,17},{17,25},{2,10},{10,18},{18,26},{... | collective-permute-start | bytes 207368 | tf_op jit(solution)/shard_map/ppermute | solution.py:24
  9.0 8.0 %copy-start.1 = (f32[2,15,32,128]{3,2,1,0:T(8,128)S(1)}, f32[2,15,32,128]{3,2,1,0:T(8,128)}, u32[]{:S(2)}) copy-start(f32[2,15,32,128]{3,2,1,0:T(8,128)} %param.7) | copy-start | bytes 1474564
  9.0 8.0 %copy-start.2 = (f32[15,32,128]{2,1,0:T(8,128)S(1)}, f32[15,32,128]{2,1,0:T(8,128)}, u32[]{:S(2)}) copy-start(f32[15,32,128]{2,1,0:T(8,128)} %param.8) | copy-start | bytes 737284
  9.5 6.6 %collective-permute-start.2 = (f32[45,38,6]{0,1,2:T(8,128)S(1)}, f32[45,38,6]{0,1,2:T(8,128)S(1)}, u32[]{:S(2)}, u32[]{:S(2)}) collective-permute-start(f32[45,38,6]{0,1,2:T(8,128)S(1)} %pad_maximum_fusion.14), channel_id=1, source_target_pairs={{0,4},{4,0},{1,5},{5,1},{2,6},{6,2},{3,7},{7,3},{8,12},{12,8},{9,1... | collective-permute-start | bytes 123128 | tf_op jit(solution)/shard_map/ppermute | solution.py:35
  23.5 8.2 %copy-start.3 = (s32[1,1024,1]{1,2,0:T(1,128)S(1)}, s32[1,1024,1]{1,2,0:T(1,128)}, u32[]{:S(2)}) copy-start(s32[1,1024,1]{1,2,0:T(1,128)} %param.10) | copy-start | bytes 12292
  25.0 14.5 %all-to-all-start = ((bf16[30,8,256]{2,0,1:T(8,128)(2,1)}), bf16[30,8,256]{2,0,1:T(8,128)(2,1)S(1)}, u32[]{:S(2)}, u32[]{:S(2)}) async-start(bf16[30,8,256]{2,0,1:T(8,128)(2,1)} %bitcast.6), calls=%async_computation | async-start | bytes 262144 | tf_op jit(solution)/shard_map/all_to_all | solution.py:149
  39.7 3.8 %copy-start.4 = (bf16[1,1024,120]{1,2,0:T(8,128)(2,1)S(1)}, bf16[1,1024,120]{1,2,0:T(8,128)(2,1)}, u32[]{:S(2)}) copy-start(bf16[1,1024,120]{1,2,0:T(8,128)(2,1)} %param.13) | copy-start | bytes 737284
  47.4 5.2 %collective-permute-start.3 = (bf16[30,1,256]{2,0,1:T(8,128)(2,1)S(1)}, bf16[30,1,256]{2,0,1:T(8,128)(2,1)S(1)}, u32[]{:S(2)}, u32[]{:S(2)}) collective-permute-start(bf16[30,1,256]{2,0,1:T(8,128)(2,1)S(1)} %bitcast.135), channel_id=1, source_target_pairs={{0,1},{1,0},{2,3},{3,2},{4,5},{5,4},{6,7},{7,6},{8,9},{9,8},{10,11... | collective-permute-start | bytes 46088 | tf_op jit(solution)/shard_map/ppermute | solution.py:169
  47.5 7.2 %collective-permute-start.4 = (bf16[30,1,256]{2,0,1:T(8,128)(2,1)S(1)}, bf16[30,1,256]{2,0,1:T(8,128)(2,1)S(1)}, u32[]{:S(2)}, u32[]{:S(2)}) collective-permute-start(bf16[30,1,256]{2,0,1:T(8,128)(2,1)S(1)} %bitcast.134), channel_id=1, source_target_pairs={{0,2},{1,3},{2,0},{3,1},{4,6},{5,7},{6,4},{7,5},{8,10},{9,11},{10,... | collective-permute-start | bytes 46088 | tf_op jit(solution)/shard_map/ppermute | solution.py:169
  48.5 10.3 %collective-permute-start.5 = (bf16[30,1,256]{2,0,1:T(8,128)(2,1)S(1)}, bf16[30,1,256]{2,0,1:T(8,128)(2,1)S(1)}, u32[]{:S(2)}, u32[]{:S(2)}) collective-permute-start(bf16[30,1,256]{2,0,1:T(8,128)(2,1)S(1)} %bitcast.133), channel_id=1, source_target_pairs={{0,3},{1,2},{2,1},{3,0},{4,7},{5,6},{6,5},{7,4},{8,11},{9,10},{10,... | collective-permute-start | bytes 46088 | tf_op jit(solution)/shard_map/ppermute | solution.py:169
  51.9 6.9 %collective-permute-start.6 = (bf16[30,1,256]{2,0,1:T(8,128)(2,1)S(1)}, bf16[30,1,256]{2,0,1:T(8,128)(2,1)S(1)}, u32[]{:S(2)}, u32[]{:S(2)}) collective-permute-start(bf16[30,1,256]{2,0,1:T(8,128)(2,1)S(1)} %bitcast.132), channel_id=1, source_target_pairs={{0,4},{1,5},{2,6},{3,7},{4,0},{5,1},{6,2},{7,3},{8,12},{9,13},{10,... | collective-permute-start | bytes 46088 | tf_op jit(solution)/shard_map/ppermute | solution.py:169
  52.5 6.3 %collective-permute-start.7 = (bf16[30,1,256]{2,0,1:T(8,128)(2,1)S(1)}, bf16[30,1,256]{2,0,1:T(8,128)(2,1)S(1)}, u32[]{:S(2)}, u32[]{:S(2)}) collective-permute-start(bf16[30,1,256]{2,0,1:T(8,128)(2,1)S(1)} %bitcast.131), channel_id=1, source_target_pairs={{0,5},{1,4},{2,7},{3,6},{4,1},{5,0},{6,3},{7,2},{8,13},{9,12},{10,... | collective-permute-start | bytes 46088 | tf_op jit(solution)/shard_map/ppermute | solution.py:169
  52.6 6.3 %collective-permute-start.8 = (bf16[30,1,256]{2,0,1:T(8,128)(2,1)S(1)}, bf16[30,1,256]{2,0,1:T(8,128)(2,1)S(1)}, u32[]{:S(2)}, u32[]{:S(2)}) collective-permute-start(bf16[30,1,256]{2,0,1:T(8,128)(2,1)S(1)} %bitcast.130), channel_id=1, source_target_pairs={{0,6},{1,7},{2,4},{3,5},{4,2},{5,3},{6,0},{7,1},{8,14},{9,15},{10,... | collective-permute-start | bytes 46088 | tf_op jit(solution)/shard_map/ppermute | solution.py:169
  54.8 6.4 %collective-permute-start.9 = (bf16[30,1,256]{2,0,1:T(8,128)(2,1)S(1)}, bf16[30,1,256]{2,0,1:T(8,128)(2,1)S(1)}, u32[]{:S(2)}, u32[]{:S(2)}) collective-permute-start(bf16[30,1,256]{2,0,1:T(8,128)(2,1)S(1)} %bitcast.129), channel_id=1, source_target_pairs={{0,7},{1,6},{2,5},{3,4},{4,3},{5,2},{6,1},{7,0},{8,15},{9,14},{10,... | collective-permute-start | bytes 46088 | tf_op jit(solution)/shard_map/ppermute | solution.py:169
